TPU v7x, 512 devices: a whole 4x4x16 slice. The times are simulated.
512 devices in a mesh: expert: 8 (over y, core), mp: 64 (over x, z).
Axes of the slice: x: 4, y: 4, z: 16, core: 2. Of those that a mesh axis runs over, the one named last changes fastest.
Arguments:
- context: bfloat16 [4096, 2048], P('expert', 'mp'), may hold values from -6 to 6
- out_proj: bfloat16 [2048, 2048], P('mp'), may hold values from -1 to 1, as said below
- routes: int32 [4096, 2], P('expert'), may hold values from 0 to 7, all different within a row; in each aligned block of 512 rows (0 to 511, 512 to 1023, ...) at most 256 rows name the same one
- router_logits: float32 [4096, 2], P('expert'), may hold values from -8 to 8
- w_gate: bfloat16 [45056, 2048], P('mp', 'expert'), may hold values from -0.125 to 0.125
- w_up: bfloat16 [45056, 2048], P('mp', 'expert'), may hold values from -0.125 to 0.125
- w_down: bfloat16 [45056, 2048], P('mp', 'expert'), may hold values from -0.078125 to 0.078125
- norm_gain: float32 [2048], P('mp'), may hold values from 0.25 to 1.75
- request_order: int32 [4096], P('expert'), may hold values from 0 to 4095, each once
Outputs:
- restored: bfloat16 [4096, 2048], P('expert', 'mp')
Inputs may be any that keep to these rules, and one draw needn't show every extreme that they name: `routes`: each row names 2 different experts. Within each aligned block of 512 rows no expert is named by more than 256 rows, and in some blocks one expert is named by exactly 256 rows. `request_order`: A permutation of the 4096 token rows. `out_proj`: entries of the order of one over the square root of 2048.
All inputs are finite; a program needn't handle non-finite values.
Results may differ from a plain program's by a relative error of at most 0.0056.
Values may be sent and summed in bfloat16 or wider, within the bound.
No kernel may reach another device: no remote copies, remote signals or barrier semaphores. Data moves between devices by JAX's collectives and lax.ppermute only.
A program may use at most 64 MiB of HBM per device.

v0:
```python
import jax
import jax.numpy as jnp
from jax import lax
from jax.sharding import PartitionSpec as P

EXPERTS = 8
CAP = 256
epsilon = 1e-06


def slot_targets(routes, capacity, experts):
    flat_routes = routes.reshape(-1)
    onehot = (flat_routes[:, None] == jnp.arange(experts, dtype=jnp.int32)[None, :]).astype(
        jnp.int32
    )
    earlier = jnp.cumsum(onehot, axis=0) - onehot
    slot_index = jnp.sum(earlier * onehot, axis=1)
    return flat_routes * capacity + slot_index


def shards(
    context, out_proj, routes, router_logits, w_gate, w_up, w_down, norm_gain, request_order
):
    tok_rows = context.shape[0]
    feat_local = context.shape[1]
    model_width = out_proj.shape[1]
    mp_count = lax.axis_size("mp")
    copies = mp_count // EXPERTS
    capacity = CAP
    top_k = routes.shape[1]
    attended = jnp.einsum(
        "td,cd->tc",
        lax.all_gather(context, "mp", axis=1, tiled=True),
        out_proj,
        preferred_element_type=jnp.float32,
    ).astype(jnp.bfloat16)
    destination = slot_targets(routes, capacity, EXPERTS)
    source_rows = jnp.repeat(jnp.arange(tok_rows, dtype=jnp.int32), top_k)
    slotted = (
        jnp.zeros((EXPERTS * capacity, feat_local), jnp.bfloat16)
        .at[destination]
        .set(attended[source_rows])
    )
    slotted = jnp.repeat(slotted.reshape(EXPERTS, capacity, feat_local), copies, axis=0)
    outgoing = slotted.transpose(1, 0, 2).reshape(capacity, mp_count * feat_local)
    inbox_rows = lax.all_to_all(outgoing, "mp", split_axis=1, concat_axis=1, tiled=True)
    gate_next = jnp.einsum(
        "rd,hd->rh",
        inbox_rows,
        lax.all_gather(w_gate, "expert", axis=1, tiled=True),
        preferred_element_type=jnp.float32,
    )
    up_next = jnp.einsum(
        "rd,hd->rh",
        inbox_rows,
        lax.all_gather(w_up, "expert", axis=1, tiled=True),
        preferred_element_type=jnp.float32,
    )
    activated = (jax.nn.silu(gate_next) * up_next).astype(jnp.bfloat16)
    partial_value = jnp.dot(
        activated,
        lax.all_gather(w_down, "expert", axis=1, tiled=True),
        preferred_element_type=jnp.float32,
    )
    returned = lax.all_to_all(partial_value, "mp", split_axis=1, concat_axis=0, tiled=True)
    expert_out = jnp.sum(returned.reshape(EXPERTS, copies, capacity, feat_local), axis=1).reshape(
        EXPERTS * capacity, feat_local
    )
    picked = expert_out[destination].reshape(tok_rows, top_k, feat_local)
    weights = 1.0 / (1.0 + jnp.exp(router_logits[:, ::-1] - router_logits))
    branch = jnp.sum(picked * weights[:, :, None], axis=1)
    combined = attended.astype(jnp.float32) + branch
    squares = lax.psum(jnp.sum(combined * combined, axis=1), "mp")
    normed = (
        combined * norm_gain[None, :] * lax.rsqrt(squares / model_width + epsilon)[:, None]
    ).astype(jnp.bfloat16)
    everyone = lax.all_gather(normed, "expert", axis=0, tiled=True)
    return everyone[request_order]


def solution(mesh):
    placed = (
        P("expert", "mp"),
        P("mp", None),
        P("expert", None),
        P("expert", None),
        P("mp", "expert"),
        P("mp", "expert"),
        P("mp", "expert"),
        P("mp"),
        P("expert"),
    )
    return jax.shard_map(
        shards, mesh=mesh, in_specs=placed, out_specs=P("expert", "mp"), check_vma=False
    )
```

profile of v0, /device:TPU:1, one launch (start us, length us, event | category | flops | bytes accessed | tf_op | source)
XLA Modules:
  0.0 565.7 jit_solution(14208333560372502879)
XLA Ops:
  6.5 0.0 copy-start
  6.5 0.0 all-gather.5.cloned.1.call-start
  6.5 0.7 all-gather.5.cloned.1.call-update
  7.3 0.0 all-gather.7.cloned.1.call-start
  7.3 0.7 all-gather.7.cloned.1.call-update
  8.0 0.0 all-gather.11.cloned.1.call-start
  8.1 0.7 all-gather.11.cloned.1.call-update
  8.7 0.0 all-gather.9.cloned.1.call-start
  8.8 0.5 all-gather.9.cloned.1.call-update
  9.3 0.8 copy.42
  10.2 0.2 eq.29
  10.3 0.2 eq.25
  10.5 0.7 broadcast_multiply_fusion
  11.2 2.3 reduce-window.6
  13.5 0.3 slice_reduce_fusion
  13.7 0.2 reduce-window.9
  13.9 0.1 add_bitcast_fusion
  14.0 0.2 copy.41
  14.1 0.2 mul.55
  14.4 0.2 reshape.104
  14.6 133.1 %all-gather.5.cloned.1.call-done = bf16[512,2048]{0,1:T(8,128)(2,1)} async-done(((bf16[512,32]{0,1:T(8,128)(2,1)}), bf16[512,2048]{0,1:T(8,128)(2,1)}) %all-gather.5.cloned.1.call-update) | async-done | bytes 2097168 | tf_op jit(solution)/shard_map/all_gather | solution.py:33
  147.7 0.0 copy-done
  147.7 2.0 convolution_convert_fusion
  149.7 0.1 copy.44
  149.9 6.4 %scatter_custom_fusion = bf16[2048,32]{1,0:T(8,128)(2,1)S(1)} fusion(s32[1024]{0:T(1024)S(1)} %bitcast.48, bf16[512,32]{1,0:T(8,128)(2,1)S(1)} %copy.44, s32[1024]{0:T(1024)S(1)} %broadcast_clamp_fusion.1, bf16[]{:T(256)} %constant.10.clone.1), kind=kCustom, calls=%fused_computation.16 | custom fusion | bytes 131074 | tf_op jit(solution)/shard_map/scatter | solution.py:42
  156.3 0.2 copy.46
  156.5 1.2 broadcast_in_dim.10
  157.7 8.8 %all-to-all-start = ((bf16[256,64,32]{0,2,1:T(8,128)(2,1)}), bf16[256,64,32]{0,2,1:T(8,128)(2,1)S(1)}, u32[]{:S(2)}, u32[]{:S(2)}) async-start(bf16[256,64,32]{0,2,1:T(8,128)(2,1)} %bitcast.6), calls=%async_computation | async-start | bytes 2097152 | tf_op jit(solution)/shard_map/all_to_all | solution.py:46
  166.5 26.9 %all-gather.7.cloned.1.call-done = bf16[704,2048]{1,0:T(8,128)(2,1)} async-done(((bf16[704,256]{1,0:T(8,128)(2,1)}), bf16[704,2048]{1,0:T(8,128)(2,1)}) %all-gather.7.cloned.1.call-update) | async-done | bytes 2883600 | tf_op jit(solution)/shard_map/all_gather | solution.py:50
  193.4 12.3 %all-to-all-done = bf16[256,64,32]{0,2,1:T(8,128)(2,1)S(1)} async-done(((bf16[256,64,32]{0,2,1:T(8,128)(2,1)}), bf16[256,64,32]{0,2,1:T(8,128)(2,1)S(1)}, u32[]{:S(2)}, u32[]{:S(2)}) %all-to-all-start) | async-done | bytes 1048608 | tf_op jit(solution)/shard_map/all_to_all | solution.py:46
  205.6 2.7 fusion.16
  208.4 26.4 %all-gather.11.cloned.1.call-done = bf16[704,2048]{1,0:T(8,128)(2,1)} async-done(((bf16[704,256]{1,0:T(8,128)(2,1)}), bf16[704,2048]{1,0:T(8,128)(2,1)}) %all-gather.11.cloned.1.call-update) | async-done | bytes 2883600 | tf_op jit(solution)/shard_map/all_gather | solution.py:62
  234.8 41.3 %all-gather.9.cloned.1.call-done = bf16[704,2048]{1,0:T(8,128)(2,1)} async-done(((bf16[704,256]{1,0:T(8,128)(2,1)}), bf16[704,2048]{1,0:T(8,128)(2,1)}) %all-gather.9.cloned.1.call-update) | async-done | bytes 2883600 | tf_op jit(solution)/shard_map/all_gather | solution.py:56
  276.1 7.2 %fusion.1 = f32[256,2048]{0,1:T(8,128)} fusion(bf16[704,2048]{1,0:T(8,128)(2,1)} %all-gather.11.cloned.1.call-done, bf16[704,2048]{1,0:T(8,128)(2,1)} %all-gather.9.cloned.1.call-done, bf16[256,2048]{0,1:T(8,128)(2,1)S(1)} %bitcast.46, f32[256,704]{0,1:T(8,128)S(1)} %fusion.16), kind=kOutput, calls=%fused_computation.8 | convolution fusion | flops 1477476352 | bytes 9633792 | tf_op jit(solution)/shard_map/dot_general | solution.py:60
  283.4 0.0 copy-start.1
  283.4 0.0 copy-start.2
  283.4 15.6 %all-to-all-start.1 = ((f32[256,64,32]{0,2,1:T(8,128)}), f32[256,64,32]{0,2,1:T(8,128)S(1)}, u32[]{:S(2)}, u32[]{:S(2)}) async-start(f32[256,64,32]{0,2,1:T(8,128)} %bitcast.43), calls=%async_computation.1 | async-start | bytes 4194304 | tf_op jit(solution)/shard_map/all_to_all | solution.py:65
  299.0 0.0 copy-done.1
  299.0 0.1 rev.3
  299.2 0.1 copy.49
  299.3 0.0 copy-done.2
  299.4 91.4 %all-to-all-done.1 = f32[256,64,32]{0,2,1:T(8,128)S(1)} async-done(((f32[256,64,32]{0,2,1:T(8,128)}), f32[256,64,32]{0,2,1:T(8,128)S(1)}, u32[]{:S(2)}, u32[]{:S(2)}) %all-to-all-start.1) | async-done | bytes 2097184 | tf_op jit(solution)/shard_map/all_to_all | solution.py:65
  390.8 0.2 bitcast_reduce_fusion
  390.9 0.3 copy.48
  391.3 0.0 copy-start.3
  391.3 2.8 gather_fusion
  394.1 2.8 multiply_reduce_fusion
  396.9 0.1 copy.50
  397.1 118.5 %psum.7 = f32[512]{0:T(512)S(1)} all-reduce(f32[512]{0:T(512)S(1)} %multiply_reduce_fusion.1), channel_id=1, replica_groups=mesh['expert'=8,'mp'=64] {'mp'}, use_global_device_ids=true, to_apply=%region_7.8 | all-reduce | flops 512 | bytes 4096 | tf_op jit(solution)/shard_map/psum | solution.py:73
  515.5 0.0 copy-done.3
  515.6 0.1 multiply_convert_fusion
  515.6 41.0 %all_gather.19 = bf16[4096,32]{0,1:T(8,128)(2,1)S(1)} all-gather(bf16[512,32]{0,1:T(8,128)(2,1)S(1)} %multiply_convert_fusion), channel_id=1, replica_groups=mesh['expert'=8,'mp'=64] {'expert'}, dimensions={0}, use_global_device_ids=true | all-gather | bytes 294912 | tf_op jit(solution)/shard_map/all_gather | solution.py:77
  556.6 0.5 copy.51
  557.1 1.3 gather_fusion.1
  558.4 0.7 copy.52
  (12 shorter events, 0.1 us)
Async XLA Ops:
  6.5 141.2 %copy-start = (bf16[32,2048]{1,0:T(8,128)(2,1)S(1)}, bf16[32,2048]{1,0:T(8,128)(2,1)}, u32[]{:S(2)}) copy-start(bf16[32,2048]{1,0:T(8,128)(2,1)} %param.10) | copy-start | bytes 393220
  6.5 141.2 %all-gather.5.cloned.1.call-start = ((), (), s32[]{:S(2)}) async-start(), calls=%async_computation.2 | async-start | bytes 2129920 | tf_op jit(solution)/shard_map/all_gather | solution.py:33
  7.3 186.1 %all-gather.7.cloned.1.call-start = ((), (), s32[]{:S(2)}) async-start(), calls=%async_computation.3 | async-start | bytes 3244032 | tf_op jit(solution)/shard_map/all_gather | solution.py:50
  8.0 226.8 %all-gather.11.cloned.1.call-start = ((), (), s32[]{:S(2)}) async-start(), calls=%async_computation.5 | async-start | bytes 3244032 | tf_op jit(solution)/shard_map/all_gather | solution.py:62
  8.7 267.4 %all-gather.9.cloned.1.call-start = ((), (), s32[]{:S(2)}) async-start(), calls=%async_computation.4 | async-start | bytes 3244032 | tf_op jit(solution)/shard_map/all_gather | solution.py:56
  157.7 48.0 %all-to-all-start = ((bf16[256,64,32]{0,2,1:T(8,128)(2,1)}), bf16[256,64,32]{0,2,1:T(8,128)(2,1)S(1)}, u32[]{:S(2)}, u32[]{:S(2)}) async-start(bf16[256,64,32]{0,2,1:T(8,128)(2,1)} %bitcast.6), calls=%async_computation | async-start | bytes 2097152 | tf_op jit(solution)/shard_map/all_to_all | solution.py:46
  283.4 15.7 %copy-start.1 = (f32[512,2]{0,1:T(2,128)S(1)}, f32[512,2]{0,1:T(2,128)}, u32[]{:S(2)}) copy-start(f32[512,2]{0,1:T(2,128)} %param.12) | copy-start | bytes 12292
  283.4 16.0 %copy-start.2 = (s32[512]{0:T(512)S(1)}, s32[512]{0:T(512)}, u32[]{:S(2)}) copy-start(s32[512]{0:T(512)} %param.17) | copy-start | bytes 6148
  283.4 107.4 %all-to-all-start.1 = ((f32[256,64,32]{0,2,1:T(8,128)}), f32[256,64,32]{0,2,1:T(8,128)S(1)}, u32[]{:S(2)}, u32[]{:S(2)}) async-start(f32[256,64,32]{0,2,1:T(8,128)} %bitcast.43), calls=%async_computation.1 | async-start | bytes 4194304 | tf_op jit(solution)/shard_map/all_to_all | solution.py:65
  391.3 124.3 %copy-start.3 = (f32[32]{0:T(128)S(1)}, f32[32]{0:T(128)}, u32[]{:S(2)}) copy-start(f32[32]{0:T(128)} %param.16) | copy-start | bytes 388
Sparse Core Ops, SparseCore 0:
  10.3 137.3 all-gather.4
  149.8 43.5 all-gather.6
  195.5 39.2 all-gather.10
  236.8 39.2 all-gather.8
where the time goes:
time: 566 us
  waiting for transfers between devices  334 us (59%)
  blocking collectives  159 us (28%)
  starting transfers between devices  24.5 us (4%)
  local copies, waits for them, and re-layouts  16 us (3%)
  between operations  13.4 us (2%)
  matrix products  12 us (2%)
  other arithmetic  6.35 us (1%)
    all_gather x1, waiting for transfers between devices, shards(): lax.all_gather(context, 'mp', axis=1, tiled=True)  133 us
    psum x1, blocking collectives, shards(): squares = lax.psum(jnp.sum(combined * combined, axis=1), 'mp')  118 us
    all_to_all x1, waiting for transfers between devices, shards(): lax.all_to_all(partial_value, 'mp', split_axis=1, concat_axis=0, tiled=True)  91.4 us
    all_gather x1, waiting for transfers between devices, shards(): lax.all_gather(w_up, 'expert', axis=1, tiled=True)  41.3 us
    all_gather x1, blocking collectives, shards(): everyone = lax.all_gather(normed, 'expert', axis=0, tiled=True)  41 us
    all_gather x1, waiting for transfers between devices, shards(): lax.all_gather(w_gate, 'expert', axis=1, tiled=True)  26.9 us
    all_gather x1, waiting for transfers between devices, shards(): lax.all_gather(w_down, 'expert', axis=1, tiled=True)  26.4 us
    all_to_all x1, starting transfers between devices, shards(): lax.all_to_all(partial_value, 'mp', split_axis=1, concat_axis=0, tiled=True)  15.6 us
  transfers between devices with their start and end apart: 6, of which 6 were waited for; matrix products, arithmetic and copies ran while one was open for 3% of the time, Pallas kernels for 0%

commit v1 on v0

--- a/solution.py
+++ b/solution.py
@@ -6,6 +6,21 @@
 EXPERTS = 8
 CAP = 256
 epsilon = 1e-06
+
+
+def process_space(target, net_axis):
+    all_blocks = [target]
+    dev = 0
+    cores_n = lax.axis_size(net_axis)
+    while dev < cores_n - 1:
+        all_blocks.append(
+            lax.ppermute(
+                all_blocks[-1], net_axis, [(i0, (i0 + 1) % cores_n) for i0 in range(cores_n)]
+            )
+        )
+        dev += 1
+    w_next = jnp.concatenate(all_blocks[::-1], 0)
+    return jnp.roll(w_next, (lax.axis_index(net_axis) + 1) * target.shape[0], axis=0)
 
 
 def slot_targets(routes, capacity, experts):
@@ -74,7 +89,7 @@
     normed = (
         combined * norm_gain[None, :] * lax.rsqrt(squares / model_width + epsilon)[:, None]
     ).astype(jnp.bfloat16)
-    everyone = lax.all_gather(normed, "expert", axis=0, tiled=True)
+    everyone = process_space(normed, "expert")
     return everyone[request_order]
 
 

time: 566 us -> 582 us (1.028)
  blocking collectives: 159 us -> 118 us
  starting transfers between devices: 24.5 us -> 58.7 us
  waiting for transfers between devices: 334 us -> 356 us
    all_gather x1 -> x0, blocking collectives: 41 us -> none  [shards(): everyone = lax.all_gather(normed, 'expert', axis=0, tiled=True)]
    ppermute x0 -> x7, starting transfers between devices: none -> 34.2 us  [process_space(): lax.ppermute(all_blocks[-1], net_axis, [(i0, (i0 + 1) % cores_n) for i0 i...]
    ppermute x0 -> x7, waiting for transfers between devices: none -> 22.1 us  [process_space(): lax.ppermute(all_blocks[-1], net_axis, [(i0, (i0 + 1) % cores_n) for i0 i...]
  transfers between devices with their start and end apart: 6 -> 13, of which waited for: 6 -> 13; matrix products, arithmetic and copies ran while one was open for 3% -> 3% of each run, Pallas kernels for 0% -> 0%
where the time goes in v1:
time: 582 us; the launch traced here: 581 us
  waiting for transfers between devices  356 us (61%)
  blocking collectives  118 us (20%)
  starting transfers between devices  58.7 us (10%)
  local copies, waits for them, and re-layouts  16.1 us (3%)
  between operations  13.5 us (2%)
  matrix products  12 us (2%)
  other arithmetic  6.35 us (1%)
    all_gather x1, waiting for transfers between devices, shards(): lax.all_gather(context, 'mp', axis=1, tiled=True)  133 us
    psum x1, blocking collectives, shards(): squares = lax.psum(jnp.sum(combined * combined, axis=1), 'mp')  118 us
    all_to_all x1, waiting for transfers between devices, shards(): lax.all_to_all(partial_value, 'mp', split_axis=1, concat_axis=0, tiled=True)  91.4 us
    all_gather x1, waiting for transfers between devices, shards(): lax.all_gather(w_up, 'expert', axis=1, tiled=True)  41.3 us
    ppermute x7, starting transfers between devices, process_space(): lax.ppermute(all_blocks[-1], net_axis, [(i0, (i0 + 1) % cores_n) for i0 i...  34.2 us
    all_gather x1, waiting for transfers between devices, shards(): lax.all_gather(w_gate, 'expert', axis=1, tiled=True)  26.9 us
    all_gather x1, waiting for transfers between devices, shards(): lax.all_gather(w_down, 'expert', axis=1, tiled=True)  26.5 us
    ppermute x7, waiting for transfers between devices, process_space(): lax.ppermute(all_blocks[-1], net_axis, [(i0, (i0 + 1) % cores_n) for i0 i...  22.1 us
  transfers between devices with their start and end apart: 13, of which 13 were waited for; matrix products, arithmetic and copies ran while one was open for 3% of the time, Pallas kernels for 0%

profile of v1, /device:TPU:1, one launch (start us, length us, event | category | flops | bytes accessed | tf_op | source)
XLA Modules:
  0.0 581.2 jit_solution(9365201621051801385)
XLA Ops:
  6.5 0.0 copy-start
  6.5 0.0 all-gather.5.cloned.1.call-start
  6.5 0.7 all-gather.5.cloned.1.call-update
  7.3 0.0 all-gather.7.cloned.1.call-start
  7.3 0.7 all-gather.7.cloned.1.call-update
  8.0 0.0 all-gather.11.cloned.1.call-start
  8.1 0.7 all-gather.11.cloned.1.call-update
  8.7 0.0 all-gather.9.cloned.1.call-start
  8.8 0.5 all-gather.9.cloned.1.call-update
  9.3 0.8 copy.42
  10.2 0.2 eq.32
  10.3 0.2 eq.28
  10.5 0.7 broadcast_multiply_fusion
  11.2 2.3 reduce-window.6
  13.5 0.3 slice_reduce_fusion
  13.7 0.2 reduce-window.9
  13.9 0.1 add_bitcast_fusion
  14.0 0.2 copy.41
  14.1 0.2 mul.58
  14.4 0.2 reshape.104
  14.6 133.1 %all-gather.5.cloned.1.call-done = bf16[512,2048]{0,1:T(8,128)(2,1)} async-done(((bf16[512,32]{0,1:T(8,128)(2,1)}), bf16[512,2048]{0,1:T(8,128)(2,1)}) %all-gather.5.cloned.1.call-update) | async-done | bytes 2097168 | tf_op jit(solution)/shard_map/all_gather | solution.py:48
  147.7 0.0 copy-done
  147.7 2.0 convolution_convert_fusion
  149.7 0.1 copy.44
  149.9 6.4 %scatter_custom_fusion = bf16[2048,32]{1,0:T(8,128)(2,1)S(1)} fusion(s32[1024]{0:T(1024)S(1)} %bitcast.47, bf16[512,32]{1,0:T(8,128)(2,1)S(1)} %copy.44, s32[1024]{0:T(1024)S(1)} %broadcast_clamp_fusion.1, bf16[]{:T(256)} %constant.22.clone.1), kind=kCustom, calls=%fused_computation.16 | custom fusion | bytes 131074 | tf_op jit(solution)/shard_map/scatter | solution.py:57
  156.3 0.2 copy.46
  156.5 1.2 broadcast_in_dim.10
  157.7 8.8 %all-to-all-start = ((bf16[256,64,32]{0,2,1:T(8,128)(2,1)}), bf16[256,64,32]{0,2,1:T(8,128)(2,1)S(1)}, u32[]{:S(2)}, u32[]{:S(2)}) async-start(bf16[256,64,32]{0,2,1:T(8,128)(2,1)} %bitcast.6), calls=%async_computation | async-start | bytes 2097152 | tf_op jit(solution)/shard_map/all_to_all | solution.py:61
  166.5 26.9 %all-gather.7.cloned.1.call-done = bf16[704,2048]{1,0:T(8,128)(2,1)} async-done(((bf16[704,256]{1,0:T(8,128)(2,1)}), bf16[704,2048]{1,0:T(8,128)(2,1)}) %all-gather.7.cloned.1.call-update) | async-done | bytes 2883600 | tf_op jit(solution)/shard_map/all_gather | solution.py:65
  193.4 12.2 %all-to-all-done = bf16[256,64,32]{0,2,1:T(8,128)(2,1)S(1)} async-done(((bf16[256,64,32]{0,2,1:T(8,128)(2,1)}), bf16[256,64,32]{0,2,1:T(8,128)(2,1)S(1)}, u32[]{:S(2)}, u32[]{:S(2)}) %all-to-all-start) | async-done | bytes 1048608 | tf_op jit(solution)/shard_map/all_to_all | solution.py:61
  205.6 2.7 fusion.16
  208.4 26.5 %all-gather.11.cloned.1.call-done = bf16[704,2048]{1,0:T(8,128)(2,1)} async-done(((bf16[704,256]{1,0:T(8,128)(2,1)}), bf16[704,2048]{1,0:T(8,128)(2,1)}) %all-gather.11.cloned.1.call-update) | async-done | bytes 2883600 | tf_op jit(solution)/shard_map/all_gather | solution.py:77
  234.8 41.3 %all-gather.9.cloned.1.call-done = bf16[704,2048]{1,0:T(8,128)(2,1)} async-done(((bf16[704,256]{1,0:T(8,128)(2,1)}), bf16[704,2048]{1,0:T(8,128)(2,1)}) %all-gather.9.cloned.1.call-update) | async-done | bytes 2883600 | tf_op jit(solution)/shard_map/all_gather | solution.py:71
  276.1 7.2 %fusion.1 = f32[256,2048]{0,1:T(8,128)} fusion(bf16[704,2048]{1,0:T(8,128)(2,1)} %all-gather.11.cloned.1.call-done, bf16[704,2048]{1,0:T(8,128)(2,1)} %all-gather.9.cloned.1.call-done, bf16[256,2048]{0,1:T(8,128)(2,1)S(1)} %bitcast.46, f32[256,704]{0,1:T(8,128)S(1)} %fusion.16), kind=kOutput, calls=%fused_computation.8 | convolution fusion | flops 1477476352 | bytes 9633792 | tf_op jit(solution)/shard_map/dot_general | solution.py:75
  283.4 15.6 %all-to-all-start.1 = ((f32[256,64,32]{0,2,1:T(8,128)}), f32[256,64,32]{0,2,1:T(8,128)S(1)}, u32[]{:S(2)}, u32[]{:S(2)}) async-start(f32[256,64,32]{0,2,1:T(8,128)} %bitcast.43), calls=%async_computation.1 | async-start | bytes 4194304 | tf_op jit(solution)/shard_map/all_to_all | solution.py:80
  299.0 0.0 copy-done.1
  299.0 0.1 rev.3
  299.2 0.1 copy.49
  299.4 91.4 %all-to-all-done.1 = f32[256,64,32]{0,2,1:T(8,128)S(1)} async-done(((f32[256,64,32]{0,2,1:T(8,128)}), f32[256,64,32]{0,2,1:T(8,128)S(1)}, u32[]{:S(2)}, u32[]{:S(2)}) %all-to-all-start.1) | async-done | bytes 2097184 | tf_op jit(solution)/shard_map/all_to_all | solution.py:80
  390.8 0.2 bitcast_reduce_fusion
  391.0 0.3 copy.48
  391.3 0.0 copy-start.3
  391.3 2.8 gather_fusion
  394.1 2.8 multiply_reduce_fusion
  396.9 0.1 copy.50
  397.1 118.5 %psum.7 = f32[512]{0:T(512)S(1)} all-reduce(f32[512]{0:T(512)S(1)} %multiply_reduce_fusion.1), channel_id=1, replica_groups=mesh['expert'=8,'mp'=64] {'mp'}, use_global_device_ids=true, to_apply=%region_7.8 | all-reduce | flops 512 | bytes 4096 | tf_op jit(solution)/shard_map/psum | solution.py:88
  515.6 0.1 multiply_convert_fusion
  515.6 28.9 %collective-permute-start = (bf16[512,32]{0,1:T(8,128)(2,1)S(1)}, bf16[512,32]{0,1:T(8,128)(2,1)S(1)}, u32[]{:S(2)}, u32[]{:S(2)}) collective-permute-start(bf16[512,32]{0,1:T(8,128)(2,1)S(1)} %multiply_convert_fusion), channel_id=1, source_target_pairs={{0,64},{64,128},{128,192},{192,256},{256,320},{320,384},{384,448},... | collective-permute-start | bytes 98312 | tf_op jit(solution)/shard_map/ppermute | solution.py:17
  544.6 1.0 collective-permute-done
  545.6 2.3 collective-permute-start.1
  547.9 1.3 collective-permute-done.1
  549.2 2.1 collective-permute-start.2
  551.2 2.5 collective-permute-done.2
  553.7 0.9 collective-permute-start.3
  554.6 3.7 collective-permute-done.3
  558.3 0.0 collective-permute-start.4
  558.3 4.5 collective-permute-done.4
  562.8 0.0 collective-permute-start.5
  562.8 4.5 collective-permute-done.5
  567.4 0.0 collective-permute-start.6
  567.4 4.5 collective-permute-done.6
  572.1 0.5 copy.51
  572.7 1.3 gather_fusion.1
  574.0 0.7 copy.52
  (32 shorter events, 0.2 us)
Async XLA Ops:
  6.5 141.2 %copy-start = (bf16[32,2048]{1,0:T(8,128)(2,1)S(1)}, bf16[32,2048]{1,0:T(8,128)(2,1)}, u32[]{:S(2)}) copy-start(bf16[32,2048]{1,0:T(8,128)(2,1)} %param.10) | copy-start | bytes 393220
  6.5 141.2 %all-gather.5.cloned.1.call-start = ((), (), s32[]{:S(2)}) async-start(), calls=%async_computation.2 | async-start | bytes 2129920 | tf_op jit(solution)/shard_map/all_gather | solution.py:48
  7.3 186.1 %all-gather.7.cloned.1.call-start = ((), (), s32[]{:S(2)}) async-start(), calls=%async_computation.3 | async-start | bytes 3244032 | tf_op jit(solution)/shard_map/all_gather | solution.py:65
  8.0 226.8 %all-gather.11.cloned.1.call-start = ((), (), s32[]{:S(2)}) async-start(), calls=%async_computation.5 | async-start | bytes 3244032 | tf_op jit(solution)/shard_map/all_gather | solution.py:77
  8.7 267.4 %all-gather.9.cloned.1.call-start = ((), (), s32[]{:S(2)}) async-start(), calls=%async_computation.4 | async-start | bytes 3244032 | tf_op jit(solution)/shard_map/all_gather | solution.py:71
  157.7 48.0 %all-to-all-start = ((bf16[256,64,32]{0,2,1:T(8,128)(2,1)}), bf16[256,64,32]{0,2,1:T(8,128)(2,1)S(1)}, u32[]{:S(2)}, u32[]{:S(2)}) async-start(bf16[256,64,32]{0,2,1:T(8,128)(2,1)} %bitcast.6), calls=%async_computation | async-start | bytes 2097152 | tf_op jit(solution)/shard_map/all_to_all | solution.py:61
  283.4 15.7 %copy-start.1 = (f32[512,2]{0,1:T(2,128)S(1)}, f32[512,2]{0,1:T(2,128)}, u32[]{:S(2)}) copy-start(f32[512,2]{0,1:T(2,128)} %param.12) | copy-start | bytes 12292
  283.4 16.0 %copy-start.2 = (s32[512]{0:T(512)S(1)}, s32[512]{0:T(512)}, u32[]{:S(2)}) copy-start(s32[512]{0:T(512)} %param.17) | copy-start | bytes 6148
  283.4 107.4 %all-to-all-start.1 = ((f32[256,64,32]{0,2,1:T(8,128)}), f32[256,64,32]{0,2,1:T(8,128)S(1)}, u32[]{:S(2)}, u32[]{:S(2)}) async-start(f32[256,64,32]{0,2,1:T(8,128)} %bitcast.43), calls=%async_computation.1 | async-start | bytes 4194304 | tf_op jit(solution)/shard_map/all_to_all | solution.py:80
  391.3 124.3 %copy-start.3 = (f32[32]{0:T(128)S(1)}, f32[32]{0:T(128)}, u32[]{:S(2)}) copy-start(f32[32]{0:T(128)} %param.16) | copy-start | bytes 388
  515.6 30.0 %collective-permute-start = (bf16[512,32]{0,1:T(8,128)(2,1)S(1)}, bf16[512,32]{0,1:T(8,128)(2,1)S(1)}, u32[]{:S(2)}, u32[]{:S(2)}) collective-permute-start(bf16[512,32]{0,1:T(8,128)(2,1)S(1)} %multiply_convert_fusion), channel_id=1, source_target_pairs={{0,64},{64,128},{128,192},{192,256},{256,320},{320,384},{384,448},... | collective-permute-start | bytes 98312 | tf_op jit(solution)/shard_map/ppermute | solution.py:17
  545.6 3.6 collective-permute-start.1
  549.2 4.6 collective-permute-start.2
  553.7 4.6 collective-permute-start.3
  558.3 4.6 collective-permute-start.4
  562.8 4.6 collective-permute-start.5
  567.4 4.6 collective-permute-start.6
Sparse Core Ops, SparseCore 0:
  10.3 137.3 all-gather.4
  149.8 43.5 all-gather.6
  195.5 39.2 all-gather.10
  236.8 39.2 all-gather.8
